TPU v7x, 128 devices: a whole 4x4x4 slice. The times are simulated.
128 devices in a mesh: dp: 8 (over x, core), pair: 16 (over z, y).
Axes of the slice: x: 4, y: 4, z: 4, core: 2. Of those that a mesh axis runs over, the one named last changes fastest.
Arguments:
- anchor: bfloat16 [5, 4096, 1024], P(None, ('dp', 'pair')), may hold values from -20 to 20
- partner: bfloat16 [5, 4096, 1024], P(None, ('dp', 'pair')), may hold values from -12 to 12
- counts: int32 [5], replicated, may hold values from 512 to 4096, as said below
- pair_scale: float32 [5], replicated, may hold values from 2 to 8
Outputs:
- loss_value: float32 [], replicated
- grad_anchor: float32 [5, 4096, 1024], P(None, ('dp', 'pair'))
- grad_partner: float32 [5, 4096, 1024], P(None, ('dp', 'pair'))
Inputs may be any that keep to these rules, and one draw needn't show every extreme that they name: The valid samples of pair p are its rows 0 to counts[p] - 1; one pair has all 4096 rows valid.
All inputs are finite; a program needn't handle non-finite values.
Results may differ from a plain program's by a relative error of at most 0.0021.
Values may be sent and summed in bfloat16 or wider, within the bound.
No kernel may reach another device: no remote copies, remote signals or barrier semaphores. Data moves between devices by JAX's collectives and lax.ppermute only.
A program may use at most 128 MiB of HBM per device.

v0:
```python
import math
import jax
import jax.numpy as jnp
from jax import lax
from jax.sharding import PartitionSpec as P

NEG = -1e30


def merge_gathered(stats):
    highs = stats[:, 0]
    sums = stats[:, 1]
    highest = jnp.max(highs, axis=0)
    summed = jnp.sum(sums * jnp.exp(highs - highest[None]), axis=0)
    return (highest, summed)


def per_device(anchor, partner, counts, pair_scale):
    pair_count, shard_rows, model_width = anchor.shape
    score_scale = 4.0 / math.sqrt(model_width)
    dp_size = lax.axis_size("dp")
    pair_size = lax.axis_size("pair")
    dp_index = lax.axis_index("dp")
    pair_place = lax.axis_index("pair")
    own_first = (dp_index * pair_size + pair_place) * shard_rows
    row_set = lax.all_gather(anchor, "pair", axis=1, tiled=True)
    col_set = lax.all_gather(partner, "dp", axis=1, tiled=True)
    row_count = row_set.shape[1]
    offsets = jnp.arange(shard_rows, dtype=jnp.int32)
    row_global = dp_index * row_count + jnp.arange(row_count, dtype=jnp.int32)
    col_first = (jnp.arange(dp_size, dtype=jnp.int32) * pair_size + pair_place) * shard_rows
    col_global = (col_first[:, None] + offsets[None, :]).reshape(-1)
    row_valid = row_global[None, :] < counts[:, None]
    col_valid = col_global[None, :] < counts[:, None]
    inside = row_valid[:, :, None] & col_valid[:, None, :]
    scores = (
        jnp.einsum("prd,pcd->prc", row_set, col_set, preferred_element_type=jnp.float32)
        * score_scale
    )
    masked = jnp.where(inside, scores, NEG)
    row_high = jnp.max(masked, axis=2)
    row_sum = jnp.sum(jnp.where(inside, jnp.exp(masked - row_high[:, :, None]), 0.0), axis=2)
    col_high = jnp.max(masked, axis=1)
    col_sum = jnp.sum(jnp.where(inside, jnp.exp(masked - col_high[:, None, :]), 0.0), axis=1)
    row_stats = lax.all_gather(jnp.stack([row_high, row_sum]), "pair")
    col_stats = lax.all_gather(jnp.stack([col_high, col_sum]), "dp")
    row_high, row_sum = merge_gathered(row_stats)
    col_high, col_sum = merge_gathered(col_stats)
    row_lse = jnp.where(row_valid, row_high + jnp.log(jnp.where(row_valid, row_sum, 1.0)), 0.0)
    col_lse = jnp.where(col_valid, col_high + jnp.log(jnp.where(col_valid, col_sum, 1.0)), 0.0)
    own_valid = own_first + offsets[None, :] < counts[:, None]
    row_own = lax.dynamic_slice_in_dim(row_lse, pair_place * shard_rows, shard_rows, 1)
    col_own = lax.dynamic_slice_in_dim(col_lse, dp_index * shard_rows, shard_rows, 1)
    positive = (
        jnp.sum(anchor.astype(jnp.float32) * partner.astype(jnp.float32), axis=2) * score_scale
    )
    loss_terms = jnp.where(own_valid, row_own + col_own - 2.0 * positive, 0.0)
    totals = lax.psum(jnp.sum(loss_terms, axis=1), ("dp", "pair"))
    loss_value = jnp.sum(totals / (2.0 * counts.astype(jnp.float32))) / pair_count
    prob_row = jnp.where(inside, jnp.exp(scores - row_lse[:, :, None]), 0.0)
    prob_col = jnp.where(inside, jnp.exp(scores - col_lse[:, None, :]), 0.0)
    weights = (pair_scale[:, None, None] * 0.5 * (prob_row + prob_col)).astype(jnp.bfloat16)
    grad_rows = (
        jnp.einsum("prc,pcd->prd", weights, col_set, preferred_element_type=jnp.float32)
        * score_scale
    )
    grad_cols = (
        jnp.einsum("prc,prd->pcd", weights, row_set, preferred_element_type=jnp.float32)
        * score_scale
    )
    anchor_part = lax.psum_scatter(grad_rows, "pair", scatter_dimension=1, tiled=True)
    partner_part = lax.psum_scatter(grad_cols, "dp", scatter_dimension=1, tiled=True)
    own_term = (pair_scale * score_scale)[:, None, None]
    keep_rows = own_valid[:, :, None]
    anchor_out = jnp.where(keep_rows, anchor_part - own_term * partner.astype(jnp.float32), 0.0)
    partner_out = jnp.where(keep_rows, partner_part - own_term * anchor.astype(jnp.float32), 0.0)
    return (loss_value, anchor_out, partner_out)


def solution(mesh):
    in_specs = (P(None, ("dp", "pair"), None), P(None, ("dp", "pair"), None), P(), P())
    out_specs = (P(), P(None, ("dp", "pair"), None), P(None, ("dp", "pair"), None))
    return jax.shard_map(
        per_device, mesh=mesh, in_specs=in_specs, out_specs=out_specs, check_vma=False
    )
```

profile of v0, /device:TPU:1, one launch (start us, length us, event | category | flops | bytes accessed | tf_op | source)
XLA Modules:
  0.0 354.5 jit_solution(2730051306671288347)
XLA Ops:
  7.2 0.0 all-gather.7.cloned.1.call-start
  7.2 0.7 all-gather.7.cloned.1.call-update
  7.9 0.0 all-gather.5.cloned.1.call-start
  7.9 0.7 all-gather.5.cloned.1.call-update
  8.6 0.0 reduce-scatter.5.cloned.1.call-start
  8.7 0.1 iota_add_fusion
  8.8 0.1 add.96
  8.9 0.7 broadcast_multiply_fusion.2
  9.5 0.7 broadcast_compare_fusion.1
  10.3 0.7 broadcast_compare_fusion
  11.0 28.5 %all-gather.7.cloned.1.call-done = bf16[5,256,1024]{2,1,0:T(8,128)(2,1)} async-done(((bf16[5,32,1024]{2,1,0:T(8,128)(2,1)}), bf16[5,256,1024]{2,1,0:T(8,128)(2,1)}) %all-gather.7.cloned.1.call-update) | async-done | bytes 2621456 | tf_op jit(solution)/shard_map/all_gather | solution.py:27
  39.4 58.8 %all-gather.5.cloned.1.call-done = bf16[5,512,1024]{2,1,0:T(8,128)(2,1)} async-done(((bf16[5,32,1024]{2,1,0:T(8,128)(2,1)}), bf16[5,512,1024]{2,1,0:T(8,128)(2,1)}) %all-gather.5.cloned.1.call-update) | async-done | bytes 5242896 | tf_op jit(solution)/shard_map/all_gather | solution.py:26
  98.2 4.9 %fusion.6 = (f32[5,512]{1,0:T(8,128)S(1)}, f32[5,256]{1,0:T(8,128)S(1)}, f32[5,512,256]{2,1,0:T(8,128)S(1)}) fusion(pred[5,256]{1,0:T(8,128)(4,1)S(1)} %broadcast_compare_fusion.1, pred[5,512]{1,0:T(8,128)(4,1)S(1)} %broadcast_compare_fusion, bf16[5,512,1024]{2,1,0:T(8,128)(2,1)} %all-gather.5.cloned.1.call-done, ...), kind=kOutput, calls=%fused_computation.13 | convolution fusion | flops 1345450240 | bytes 10504960 | tf_op jit(solution)/shard_map/prd,pcd->prc/dot_general | solution.py:37
  103.2 0.0 copy-start.2
  103.2 2.0 fusion
  105.2 13.6 %all-gather.1 = f32[16,5,256]{2,1,0:T(8,128)S(1)} all-gather(f32[2,5,256]{2,1,0:T(8,128)S(1)} %pad_maximum_fusion.1), channel_id=3, replica_groups=mesh['dp'=8,'pair'=16] {'dp'}, dimensions={0}, use_global_device_ids=true | all-gather | bytes 92160 | tf_op jit(solution)/shard_map/all_gather | solution.py:46
  118.9 0.1 add_select_fusion.1
  119.0 18.7 %all-gather = f32[32,5,512]{2,1,0:T(8,128)S(1)} all-gather(f32[2,5,512]{2,1,0:T(8,128)S(1)} %pad_maximum_fusion), channel_id=2, replica_groups=mesh['dp'=8,'pair'=16] {'pair'}, dimensions={0}, use_global_device_ids=true | all-gather | bytes 348160 | tf_op jit(solution)/shard_map/all_gather | solution.py:45
  137.7 0.1 fusion.13
  137.8 0.1 add_select_fusion
  137.8 5.1 %broadcast_multiply_fusion.1 = f32[5,256,1024]{2,1,0:T(8,128)} fusion(bf16[5,512,1024]{2,1,0:T(8,128)(2,1)S(1)} %copy-done.3, f32[5,512,256]{2,1,0:T(8,128)S(1)} %get-tuple-element.12, f32[5,256]{1,0:T(8,128)S(1)} %add_select_fusion.1, f32[5,512]{1,0:T(8,128)S(1)} %add_select_fusion, f32[5]{0:T(128)S(1)} %get-tuple-element.11, ...), kind=kOutput, calls=%fused_computation.11 | convolution fusion | flops 1349386240 | bytes 13126420 | tf_op jit(solution)/shard_map/prc,prd->pcd/dot_general | solution.py:68
  142.9 0.0 reduce-scatter.5.cloned.1.call-update
  142.9 0.0 reduce-scatter.3.cloned.1.call-start
  143.0 7.6 %broadcast_multiply_fusion = f32[5,512,1024]{2,1,0:T(8,128)} fusion(bf16[5,256,1024]{2,1,0:T(8,128)(2,1)} %all-gather.7.cloned.1.call-done, f32[5,512,256]{2,1,0:T(8,128)S(1)} %get-tuple-element.12, f32[5,256]{1,0:T(8,128)S(1)} %add_select_fusion.1, f32[5,512]{1,0:T(8,128)S(1)} %add_select_fusion, f32[5]{0:T(128)S(1)} %get-tuple-element.11, ...), kind=kOutput, calls=%fused_computation.5 | convolution fusion | flops 1350696960 | bytes 15747860 | tf_op jit(solution)/shard_map/prc,pcd->prd/dot_general | solution.py:64
  150.6 0.0 reduce-scatter.3.cloned.1.call-update
  150.6 0.1 broadcast_compare_fusion.2
  150.7 32.2 %reduce-scatter.5.cloned.1.call-done = f32[5,32,1024]{2,1,0:T(8,128)} async-done(((f32[5,256,1024]{2,1,0:T(8,128)}), f32[5,32,1024]{2,1,0:T(8,128)}) %reduce-scatter.5.cloned.1.call-update) | async-done | bytes 655376 | tf_op jit(solution)/shard_map/reduce_scatter | solution.py:72
  182.9 94.8 %reduce-scatter.3.cloned.1.call-done = f32[5,32,1024]{2,1,0:T(8,128)} async-done(((f32[5,512,1024]{2,1,0:T(8,128)}), f32[5,32,1024]{2,1,0:T(8,128)}) %reduce-scatter.3.cloned.1.call-update) | async-done | bytes 655376 | tf_op jit(solution)/shard_map/reduce_scatter | solution.py:71
  277.7 2.7 fusion.8
  280.4 0.2 select_reduce_fusion
  280.6 65.0 %psum.7 = f32[5]{0:T(128)S(1)} all-reduce(f32[5]{0:T(128)S(1)} %select_reduce_fusion), channel_id=1, replica_groups=mesh['dp'=8,'pair'=16] {'dp','pair'}, use_global_device_ids=true, to_apply=%region_10.11 | all-reduce | flops 5 | bytes 40 | tf_op jit(solution)/shard_map/psum | solution.py:58
  345.6 0.6 fusion.18
  (15 shorter events, 0.1 us)
Async XLA Ops:
  7.2 32.3 %all-gather.7.cloned.1.call-start = ((), (), s32[]{:S(2)}) async-start(), calls=%async_computation.3 | async-start | bytes 2949120 | tf_op jit(solution)/shard_map/all_gather | solution.py:27
  7.9 90.3 %all-gather.5.cloned.1.call-start = ((), (), s32[]{:S(2)}) async-start(), calls=%async_computation.2 | async-start | bytes 5570560 | tf_op jit(solution)/shard_map/all_gather | solution.py:26
  8.6 174.2 %reduce-scatter.5.cloned.1.call-start = ((), (), s32[]{:S(2)}) async-start(), calls=%async_computation.5 | async-start | bytes 5898240 | tf_op jit(solution)/shard_map/reduce_scatter | solution.py:72
  98.2 39.6 %copy-start.3 = (bf16[5,512,1024]{2,1,0:T(8,128)(2,1)S(1)}, bf16[5,512,1024]{2,1,0:T(8,128)(2,1)}, u32[]{:S(2)}) copy-start(bf16[5,512,1024]{2,1,0:T(8,128)(2,1)} %all-gather.5.cloned.1.call-done) | copy-start | bytes 15728644
  103.2 15.7 %copy-start.2 = (s32[5]{0:T(128)S(1)}, s32[5]{0:T(128)}, u32[]{:S(2)}) copy-start(s32[5]{0:T(128)} %param.6) | copy-start | bytes 64
  142.9 134.8 %reduce-scatter.3.cloned.1.call-start = ((), (), s32[]{:S(2)}) async-start(), calls=%async_computation.4 | async-start | bytes 11141120 | tf_op jit(solution)/shard_map/reduce_scatter | solution.py:71
  150.5 127.1 %copy-start = (bf16[5,32,1024]{2,1,0:T(8,128)(2,1)S(1)}, bf16[5,32,1024]{2,1,0:T(8,128)(2,1)}, u32[]{:S(2)}) copy-start(bf16[5,32,1024]{2,1,0:T(8,128)(2,1)} %param.5) | copy-start | bytes 983044
  150.5 127.1 %copy-start.1 = (bf16[5,32,1024]{2,1,0:T(8,128)(2,1)S(1)}, bf16[5,32,1024]{2,1,0:T(8,128)(2,1)}, u32[]{:S(2)}) copy-start(bf16[5,32,1024]{2,1,0:T(8,128)(2,1)} %param.4) | copy-start | bytes 983044
Sparse Core Ops, SparseCore 0:
  9.7 29.7 all-gather.6
  41.6 56.6 all-gather.4
  143.0 39.7 reduce-scatter.4
  186.2 91.4 reduce-scatter.2
where the time goes:
time: 355 us
  waiting for transfers between devices  216 us (61%)
  blocking collectives  97.3 us (27%)
  matrix products  17.6 us (5%)
  between operations  15.6 us (4%)
  other arithmetic  8.11 us (2%)
    reduce_scatter x1, waiting for transfers between devices, per_device(): lax.psum_scatter(grad_rows, 'pair', scatter_dimension=1, tiled=True)  94.8 us
    psum x1, blocking collectives, per_device(): totals = lax.psum(jnp.sum(loss_terms, axis=1), ('dp', 'pair'))  65 us
    all_gather x1, waiting for transfers between devices, per_device(): row_set = lax.all_gather(anchor, 'pair', axis=1, tiled=True)  58.8 us
    reduce_scatter x1, waiting for transfers between devices, per_device(): lax.psum_scatter(grad_cols, 'dp', scatter_dimension=1, tiled=True)  32.2 us
    all_gather x1, waiting for transfers between devices, per_device(): col_set = lax.all_gather(partner, 'dp', axis=1, tiled=True)  28.5 us
    all_gather x1, blocking collectives, per_device(): row_stats = lax.all_gather(jnp.stack([row_high, row_sum]), 'pair')  18.7 us
    all_gather x1, blocking collectives, per_device(): col_stats = lax.all_gather(jnp.stack([col_high, col_sum]), 'dp')  13.6 us
    dot_general x1, matrix products, per_device(): jnp.einsum('prc,pcd->prd', weights, col_set, preferred_element_type=jnp.f...  7.57 us
  transfers between devices with their start and end apart: 4, of which 4 were waited for; matrix products, arithmetic and copies ran while one was open for 3% of the time, Pallas kernels for 0%

commit v1 on v0

--- a/solution.py
+++ b/solution.py
@@ -55,7 +55,7 @@
         jnp.sum(anchor.astype(jnp.float32) * partner.astype(jnp.float32), axis=2) * score_scale
     )
     loss_terms = jnp.where(own_valid, row_own + col_own - 2.0 * positive, 0.0)
-    totals = lax.psum(jnp.sum(loss_terms, axis=1), ("dp", "pair"))
+    totals = lax.psum(lax.psum(jnp.sum(loss_terms, axis=1), "pair"), "dp")
     loss_value = jnp.sum(totals / (2.0 * counts.astype(jnp.float32))) / pair_count
     prob_row = jnp.where(inside, jnp.exp(scores - row_lse[:, :, None]), 0.0)
     prob_col = jnp.where(inside, jnp.exp(scores - col_lse[:, None, :]), 0.0)

time: 355 us -> 341 us (0.961)
  blocking collectives: 97.3 us -> 83.5 us
    psum x1 -> x2, blocking collectives: 65 us -> 51.3 us  [per_device(): totals = lax.psum(lax.psum(jnp.sum(loss_terms, axis=1), 'pair'), 'dp')]
where the time goes in v1:
time: 341 us
  waiting for transfers between devices  216 us (63%)
  blocking collectives  83.5 us (24%)
  matrix products  17.6 us (5%)
  between operations  15.6 us (5%)
  other arithmetic  8.11 us (2%)
    reduce_scatter x1, waiting for transfers between devices, per_device(): lax.psum_scatter(grad_rows, 'pair', scatter_dimension=1, tiled=True)  94.8 us
    all_gather x1, waiting for transfers between devices, per_device(): row_set = lax.all_gather(anchor, 'pair', axis=1, tiled=True)  58.8 us
    psum x2, blocking collectives, per_device(): totals = lax.psum(lax.psum(jnp.sum(loss_terms, axis=1), 'pair'), 'dp')  51.3 us
    reduce_scatter x1, waiting for transfers between devices, per_device(): lax.psum_scatter(grad_cols, 'dp', scatter_dimension=1, tiled=True)  32.2 us
    all_gather x1, waiting for transfers between devices, per_device(): col_set = lax.all_gather(partner, 'dp', axis=1, tiled=True)  28.5 us
    all_gather x1, blocking collectives, per_device(): row_stats = lax.all_gather(jnp.stack([row_high, row_sum]), 'pair')  18.7 us
    all_gather x1, blocking collectives, per_device(): col_stats = lax.all_gather(jnp.stack([col_high, col_sum]), 'dp')  13.6 us
    dot_general x1, matrix products, per_device(): jnp.einsum('prc,pcd->prd', weights, col_set, preferred_element_type=jnp.f...  7.57 us
  transfers between devices with their start and end apart: 4, of which 4 were waited for; matrix products, arithmetic and copies ran while one was open for 3% of the time, Pallas kernels for 0%

profile of v1, /device:TPU:1, one launch (start us, length us, event | category | flops | bytes accessed | tf_op | source)
XLA Modules:
  0.0 340.8 jit_solution(11090121848938104500)
XLA Ops:
  7.2 0.0 all-gather.7.cloned.1.call-start
  7.2 0.7 all-gather.7.cloned.1.call-update
  7.9 0.0 all-gather.5.cloned.1.call-start
  7.9 0.7 all-gather.5.cloned.1.call-update
  8.6 0.0 reduce-scatter.5.cloned.1.call-start
  8.7 0.1 iota_add_fusion
  8.8 0.1 add.98
  8.9 0.7 broadcast_multiply_fusion.2
  9.5 0.7 broadcast_compare_fusion.1
  10.3 0.7 broadcast_compare_fusion
  11.0 28.5 %all-gather.7.cloned.1.call-done = bf16[5,256,1024]{2,1,0:T(8,128)(2,1)} async-done(((bf16[5,32,1024]{2,1,0:T(8,128)(2,1)}), bf16[5,256,1024]{2,1,0:T(8,128)(2,1)}) %all-gather.7.cloned.1.call-update) | async-done | bytes 2621456 | tf_op jit(solution)/shard_map/all_gather | solution.py:27
  39.4 58.8 %all-gather.5.cloned.1.call-done = bf16[5,512,1024]{2,1,0:T(8,128)(2,1)} async-done(((bf16[5,32,1024]{2,1,0:T(8,128)(2,1)}), bf16[5,512,1024]{2,1,0:T(8,128)(2,1)}) %all-gather.5.cloned.1.call-update) | async-done | bytes 5242896 | tf_op jit(solution)/shard_map/all_gather | solution.py:26
  98.2 4.9 %fusion.6 = (f32[5,512]{1,0:T(8,128)S(1)}, f32[5,256]{1,0:T(8,128)S(1)}, f32[5,512,256]{2,1,0:T(8,128)S(1)}) fusion(pred[5,256]{1,0:T(8,128)(4,1)S(1)} %broadcast_compare_fusion.1, pred[5,512]{1,0:T(8,128)(4,1)S(1)} %broadcast_compare_fusion, bf16[5,512,1024]{2,1,0:T(8,128)(2,1)} %all-gather.5.cloned.1.call-done, ...), kind=kOutput, calls=%fused_computation.13 | convolution fusion | flops 1345450240 | bytes 10504960 | tf_op jit(solution)/shard_map/prd,pcd->prc/dot_general | solution.py:37
  103.2 2.0 fusion
  105.2 13.6 %all-gather.1 = f32[16,5,256]{2,1,0:T(8,128)S(1)} all-gather(f32[2,5,256]{2,1,0:T(8,128)S(1)} %pad_maximum_fusion.1), channel_id=3, replica_groups=mesh['dp'=8,'pair'=16] {'dp'}, dimensions={0}, use_global_device_ids=true | all-gather | bytes 92160 | tf_op jit(solution)/shard_map/all_gather | solution.py:46
  118.9 0.1 add_select_fusion.1
  119.0 18.7 %all-gather = f32[32,5,512]{2,1,0:T(8,128)S(1)} all-gather(f32[2,5,512]{2,1,0:T(8,128)S(1)} %pad_maximum_fusion), channel_id=2, replica_groups=mesh['dp'=8,'pair'=16] {'pair'}, dimensions={0}, use_global_device_ids=true | all-gather | bytes 348160 | tf_op jit(solution)/shard_map/all_gather | solution.py:45
  137.7 0.1 fusion.13
  137.8 0.1 add_select_fusion
  137.8 5.1 %broadcast_multiply_fusion.1 = f32[5,256,1024]{2,1,0:T(8,128)} fusion(bf16[5,512,1024]{2,1,0:T(8,128)(2,1)S(1)} %copy-done.3, f32[5,512,256]{2,1,0:T(8,128)S(1)} %get-tuple-element.12, f32[5,256]{1,0:T(8,128)S(1)} %add_select_fusion.1, f32[5,512]{1,0:T(8,128)S(1)} %add_select_fusion, f32[5]{0:T(128)S(1)} %get-tuple-element.11, ...), kind=kOutput, calls=%fused_computation.11 | convolution fusion | flops 1349386240 | bytes 13126420 | tf_op jit(solution)/shard_map/prc,prd->pcd/dot_general | solution.py:68
  142.9 0.0 reduce-scatter.5.cloned.1.call-update
  142.9 0.0 reduce-scatter.3.cloned.1.call-start
  143.0 7.6 %broadcast_multiply_fusion = f32[5,512,1024]{2,1,0:T(8,128)} fusion(bf16[5,256,1024]{2,1,0:T(8,128)(2,1)} %all-gather.7.cloned.1.call-done, f32[5,512,256]{2,1,0:T(8,128)S(1)} %get-tuple-element.12, f32[5,256]{1,0:T(8,128)S(1)} %add_select_fusion.1, f32[5,512]{1,0:T(8,128)S(1)} %add_select_fusion, f32[5]{0:T(128)S(1)} %get-tuple-element.11, ...), kind=kOutput, calls=%fused_computation.5 | convolution fusion | flops 1350696960 | bytes 15747860 | tf_op jit(solution)/shard_map/prc,pcd->prd/dot_general | solution.py:64
  150.6 0.0 reduce-scatter.3.cloned.1.call-update
  150.6 0.1 broadcast_compare_fusion.2
  150.7 32.2 %reduce-scatter.5.cloned.1.call-done = f32[5,32,1024]{2,1,0:T(8,128)} async-done(((f32[5,256,1024]{2,1,0:T(8,128)}), f32[5,32,1024]{2,1,0:T(8,128)}) %reduce-scatter.5.cloned.1.call-update) | async-done | bytes 655376 | tf_op jit(solution)/shard_map/reduce_scatter | solution.py:72
  182.9 94.8 %reduce-scatter.3.cloned.1.call-done = f32[5,32,1024]{2,1,0:T(8,128)} async-done(((f32[5,512,1024]{2,1,0:T(8,128)}), f32[5,32,1024]{2,1,0:T(8,128)}) %reduce-scatter.3.cloned.1.call-update) | async-done | bytes 655376 | tf_op jit(solution)/shard_map/reduce_scatter | solution.py:71
  277.7 2.7 fusion.8
  280.4 0.2 select_reduce_fusion
  280.6 30.9 %psum.14 = f32[5]{0:T(128)S(1)} all-reduce(f32[5]{0:T(128)S(1)} %select_reduce_fusion), channel_id=1, replica_groups=mesh['dp'=8,'pair'=16] {'pair'}, use_global_device_ids=true, to_apply=%region_10.11 | all-reduce | flops 5 | bytes 40 | tf_op jit(solution)/shard_map/psum | solution.py:58
  311.5 20.4 %psum.15 = f32[5]{0:T(128)S(1)} all-reduce(f32[5]{0:T(128)S(1)} %psum.14), channel_id=1, replica_groups=mesh['dp'=8,'pair'=16] {'dp'}, use_global_device_ids=true, to_apply=%region_11.12 | all-reduce | flops 5 | bytes 40 | tf_op jit(solution)/shard_map/psum | solution.py:58
  331.9 0.6 fusion.18
  (16 shorter events, 0.1 us)
Async XLA Ops:
  7.2 32.3 %all-gather.7.cloned.1.call-start = ((), (), s32[]{:S(2)}) async-start(), calls=%async_computation.3 | async-start | bytes 2949120 | tf_op jit(solution)/shard_map/all_gather | solution.py:27
  7.9 90.3 %all-gather.5.cloned.1.call-start = ((), (), s32[]{:S(2)}) async-start(), calls=%async_computation.2 | async-start | bytes 5570560 | tf_op jit(solution)/shard_map/all_gather | solution.py:26
  8.6 174.2 %reduce-scatter.5.cloned.1.call-start = ((), (), s32[]{:S(2)}) async-start(), calls=%async_computation.5 | async-start | bytes 5898240 | tf_op jit(solution)/shard_map/reduce_scatter | solution.py:72
  98.2 39.6 %copy-start.3 = (bf16[5,512,1024]{2,1,0:T(8,128)(2,1)S(1)}, bf16[5,512,1024]{2,1,0:T(8,128)(2,1)}, u32[]{:S(2)}) copy-start(bf16[5,512,1024]{2,1,0:T(8,128)(2,1)} %all-gather.5.cloned.1.call-done) | copy-start | bytes 15728644
  103.2 15.7 %copy-start.2 = (s32[5]{0:T(128)S(1)}, s32[5]{0:T(128)}, u32[]{:S(2)}) copy-start(s32[5]{0:T(128)} %param.6) | copy-start | bytes 64
  142.9 134.8 %reduce-scatter.3.cloned.1.call-start = ((), (), s32[]{:S(2)}) async-start(), calls=%async_computation.4 | async-start | bytes 11141120 | tf_op jit(solution)/shard_map/reduce_scatter | solution.py:71
  150.5 127.1 %copy-start = (bf16[5,32,1024]{2,1,0:T(8,128)(2,1)S(1)}, bf16[5,32,1024]{2,1,0:T(8,128)(2,1)}, u32[]{:S(2)}) copy-start(bf16[5,32,1024]{2,1,0:T(8,128)(2,1)} %param.5) | copy-start | bytes 983044
  150.5 127.1 %copy-start.1 = (bf16[5,32,1024]{2,1,0:T(8,128)(2,1)S(1)}, bf16[5,32,1024]{2,1,0:T(8,128)(2,1)}, u32[]{:S(2)}) copy-start(bf16[5,32,1024]{2,1,0:T(8,128)(2,1)} %param.4) | copy-start | bytes 983044
Sparse Core Ops, SparseCore 0:
  9.7 29.7 all-gather.6
  41.6 56.6 all-gather.4
  143.0 39.7 reduce-scatter.4
  186.2 91.4 reduce-scatter.2
